TPU v7x, 512 devices: a whole 4x4x16 slice. The times are simulated.
512 devices in a mesh: pipe: 16 (over z_hi, y), zero: 32 (over z_lo, x, core).
Axes of the slice: x: 4, y: 4, z: 16 (z_hi: 4, z_lo: 4; z = z_hi * 4 + z_lo), core: 2. Of those that a mesh axis runs over, the one named last changes fastest.
Arguments:
- residual: bfloat16 [16, 2048, 4096], P('pipe', 'zero'), may hold values from -6 to 6
- norm_gain: bfloat16 [16, 4096], P('pipe'), may hold values from 0.099609375 to 1.8984375
- queries: bfloat16 [16, 2048, 4096], P('pipe', 'zero'), may hold values from -74 to 74
- cached_kv: bfloat16 [16, 512, 1024], P('pipe', 'zero'), may hold values from -6 to 6
- panel_blocks: bfloat16 [16, 160, 128, 128], P('pipe', 'zero'), may hold values from -0.125 to 0.125
- block_rows: int32 [16, 8, 20], P('pipe'), may hold values from 0 to 31, as said below
- counts: int32 [16, 8], P('pipe'), may hold values from 12 to 20, as said below
Outputs:
- passed: bfloat16 [16, 2048, 4096], P('pipe', 'zero')
- new_kv: bfloat16 [16, 2048, 1024], P('pipe', 'zero')
Inputs may be any that keep to these rules, and one draw needn't show every extreme that they name: `block_rows`: row blocks named by the slots of one panel are all different. `counts`: slots at or beyond a panel's count are padding.
All inputs are finite; a program needn't handle non-finite values.
Results may differ from a plain program's by a relative error of at most 0.0047.
The roundings to bfloat16 on the way count: a program that leaves them out, or rounds other values in their place, can miss the bound.
Values may be sent and summed in bfloat16 or wider, within the bound.
No kernel may reach another device: no remote copies, remote signals or barrier semaphores. Data moves between devices by JAX's collectives and lax.ppermute only.
A program may use at most 64 MiB of HBM per device.

v0:
```python
import math
import jax
import jax.numpy as jnp
from jax import lax
from jax.sharding import PartitionSpec as P

QH = 32
KVH = 4
HD = 128


def passed_along(block, axis, distance):
    devices = range(lax.axis_size(axis))
    route = [((i - distance) % len(devices), i) for i in devices]
    return lax.ppermute(block, axis, route)


def local(residual, norm_gain, queries, cached_kv, panel_blocks, block_rows, counts):
    row_count = residual.shape[1]
    model_width = residual.shape[2]
    zero_index = lax.axis_index("zero")
    stream = residual[0].astype(jnp.float32)
    normed = (
        stream
        * lax.rsqrt(jnp.mean(stream * stream, axis=-1, keepdims=True) + 1e-05)
        * norm_gain[0].astype(jnp.float32)
    ).astype(jnp.bfloat16)
    block_size = panel_blocks.shape[-1]
    panels = block_rows.shape[1]
    slot_depth = block_rows.shape[2]
    row_table = block_rows[0].reshape(-1)
    slot_live = (
        (jnp.arange(slot_depth)[None, :] < counts[0][:, None]).astype(jnp.float32).reshape(-1)
    )
    normed_grid = normed.reshape(row_count, model_width // block_size, block_size)
    kv_heads = KVH
    head_size = HD
    group_size = QH // KVH
    kv_width = kv_heads * head_size
    score_scale = 1.0 / math.sqrt(head_size)
    query_grid = queries[0].reshape(row_count, kv_heads, group_size, head_size)
    first_query = zero_index * row_count
    query_pos = first_query + jnp.arange(row_count)
    initial = (
        jnp.full((kv_heads, row_count, group_size), -1e30, jnp.float32),
        jnp.zeros((kv_heads, row_count, group_size), jnp.float32),
        jnp.zeros((kv_heads, row_count, group_size, head_size), jnp.float32),
    )

    def absorb(running, portion, visible):
        run_max, run_sum, run_acc = running
        key_count = portion.shape[0]
        key_grid = portion[:, :kv_width].reshape(key_count, kv_heads, head_size)
        value_grid = portion[:, kv_width:].reshape(key_count, kv_heads, head_size)
        scores = (
            jnp.einsum("rgjd,ngd->grjn", query_grid, key_grid, preferred_element_type=jnp.float32)
            * score_scale
        )
        visible_mask = visible[None, :, None, :]
        new_max = jnp.maximum(run_max, jnp.max(jnp.where(visible_mask, scores, -1e30), axis=-1))
        shrink = jnp.exp(run_max - new_max)
        weights = jnp.where(visible_mask, jnp.exp(scores - new_max[..., None]), 0.0)
        new_sum = run_sum * shrink + jnp.sum(weights, axis=-1)
        new_acc = run_acc * shrink[..., None] + jnp.einsum(
            "grjn,ngd->grjd",
            weights.astype(jnp.bfloat16),
            value_grid,
            preferred_element_type=jnp.float32,
        )
        return (new_max, new_sum, new_acc)

    zero_size = lax.axis_size("zero")
    local_slots = panel_blocks.shape[1]
    weight_rows = local_slots * block_size
    cache_local = cached_kv[0].reshape(-1, block_size)
    packed = jnp.concatenate(
        [panel_blocks[0].reshape(weight_rows, block_size), cache_local], axis=0
    )
    gathered = lax.all_gather(packed, "zero", axis=0, tiled=True).reshape(
        zero_size, packed.shape[0], block_size
    )
    all_blocks = gathered[:, :weight_rows].reshape(zero_size * local_slots, block_size, block_size)
    cache_portion = gathered[:, weight_rows:].reshape(
        zero_size * cached_kv.shape[1], cached_kv.shape[2]
    )
    chosen = jnp.take(normed_grid, row_table, axis=1)
    slot_terms = jnp.einsum("rsk,skn->rsn", chosen, all_blocks, preferred_element_type=jnp.float32)
    slot_terms = slot_terms * slot_live[None, :, None]
    summed = slot_terms.reshape(row_count, panels, slot_depth, block_size).sum(axis=2)
    kv_new = summed.reshape(row_count, panels * block_size).astype(jnp.bfloat16)
    softmax_state = absorb(
        initial, cache_portion, jnp.ones((row_count, cache_portion.shape[0]), bool)
    )
    portion = lax.all_gather(kv_new, "zero", axis=0, tiled=True)
    key_pos = jnp.arange(portion.shape[0])
    visible = key_pos[None, :] <= query_pos[:, None]
    softmax_state = lax.cond(
        jnp.int32(0) <= first_query + row_count - 1,
        lambda state_in: absorb(state_in, portion, visible),
        lambda state_in: state_in,
        softmax_state,
    )
    run_max, denominator, run_acc = softmax_state
    attended = run_acc / denominator[..., None]
    attended = jnp.transpose(attended, (1, 0, 2, 3)).reshape(
        row_count, kv_heads * group_size * head_size
    )
    updated = (stream + attended).astype(jnp.bfloat16)
    passed = passed_along(updated[None], "pipe", 1)
    return (passed, kv_new[None])


def solution(mesh):
    in_specs = (
        P("pipe", "zero", None),
        P("pipe", None),
        P("pipe", "zero", None),
        P("pipe", "zero", None),
        P("pipe", "zero", None, None),
        P("pipe", None, None),
        P("pipe", None),
    )
    out_specs = (P("pipe", "zero", None), P("pipe", "zero", None))
    return jax.shard_map(local, mesh=mesh, in_specs=in_specs, out_specs=out_specs, check_vma=False)
```

profile of v0, /device:TPU:96, one launch (start us, length us, event | category | flops | bytes accessed | tf_op | source)
XLA Modules:
  0.0 260.9 jit_solution(13501119565918339690)
XLA Ops:
  7.2 0.0 all-gather.3.cloned.1.call-start
  7.2 0.8 reshape_squeeze.15
  8.1 1.6 pad_maximum_fusion
  9.7 0.0 all-gather.3.cloned.1.call-update
  9.7 0.0 all-gather.5.cloned.1.call-start
  9.8 0.8 reshape_squeeze.18
  10.5 0.8 reshape_squeeze.17
  11.3 1.1 convert_bitcast_fusion
  12.4 0.2 copy.84
  12.6 0.1 fusion.33
  12.7 0.1 reshape.143
  12.8 0.2 fusion.27
  13.0 0.7 fusion.30
  13.7 1.1 gather_fusion
  14.8 68.7 %all-gather.3.cloned.1.call-done = bf16[24576,128]{1,0:T(8,128)(2,1)} async-done(((bf16[768,128]{1,0:T(8,128)(2,1)}), bf16[24576,128]{1,0:T(8,128)(2,1)}) %all-gather.3.cloned.1.call-update) | async-done | bytes 6291472 | tf_op jit(solution)/shard_map/all_gather | solution.py:79
  83.5 2.8 %slice.29 = bf16[32,640,128]{2,1,0:T(8,128)(2,1)S(1)} slice(bf16[32,768,128]{2,1,0:T(8,128)(2,1)} %bitcast.70), slice={[0:32], [0:640], [0:128]} | slice | bytes 10485760 | tf_op jit(solution)/shard_map/slice | solution.py:82
  86.4 3.7 %broadcast_multiply_fusion = f32[160,128,64]{1,2,0:T(8,128)} fusion(f32[160]{0:T(256)S(1)} %reshape.143, bf16[160,128,128]{2,1,0:T(8,128)(2,1)S(1)} %bitcast.68, bf16[160,64,128]{2,1,0:T(8,128)(2,1)S(1)} %gather_fusion, pred[160]{0:T(512)(128)(4,1)S(1)} %compare_and_fusion), kind=kOutput, calls=%fused_computation.24 | convolution fusion | flops 338165760 | bytes 13108000 | tf_op jit(solution)/shard_map/rsk,skn->rsn/dot_general | solution.py:87
  90.1 3.0 %reduce_sum.38 = bf16[64,8,128]{2,0,1:T(8,128)(2,1)S(1)} reduce(f32[64,8,20,128]{3,0,2,1:T(8,128)} %bitcast.67, f32[]{:T(128)} %constant.28.clone.1), dimensions={2}, to_apply=%region_3.4 | reduce | flops 1245184 | bytes 5373956 | tf_op jit(solution)/shard_map/reduce_sum | solution.py:89
  93.1 0.7 copy_bitcast_fusion
  93.8 0.1 copy.83
  93.9 1.3 slice.26
  95.2 0.5 reshape.135
  95.7 0.1 fusion.37
  95.8 0.2 copy.54
  96.0 0.8 bitcast_reduce_fusion
  96.8 1.1 fusion.13
  97.9 0.1 copy.57
  98.0 1.0 copy.58
  99.0 3.4 %fusion.23 = f32[4,64,8,128]{3,2,1,0:T(8,128)} fusion(bf16[512,4,128,1]{0,2,3,1:T(8,128)(2,1)} %bitcast.78, bf16[4,64,8,512]{3,1,2,0:T(8,128)(2,1)S(1)} %get-tuple-element.81, f32[4,64,8]{2,1,0:T(8,128)S(1)} %copy.57), kind=kOutput, calls=%fused_computation.31 | convolution fusion | flops 268697600 | bytes 3678208 | tf_op jit(solution)/shard_map/grjn,ngd->grjd/dot_general | solution.py:64
  102.4 58.1 %all-gather.5.cloned.1.call-done = bf16[2048,1024]{1,0:T(8,128)(2,1)} async-done(((bf16[64,1024]{1,0:T(8,128)(2,1)}), bf16[2048,1024]{1,0:T(8,128)(2,1)}) %all-gather.5.cloned.1.call-update) | async-done | bytes 4194320 | tf_op jit(solution)/shard_map/all_gather | solution.py:94
  160.5 34.9 %conditional.1 = (f32[4,64,8]{2,1,0:T(8,128)S(1)}, f32[4,64,8,128]{3,2,1,0:T(8,128)}) conditional(s32[]{:T(128)} %convert_element_type.57, (f32[4,64,8]{1,2,0:T(8,128)S(1)}, f32[4,64,8,128]{3,2,1,0:T(8,128)}) %tuple.15, (s32[]{:T(128)}, s32[64,1]{0,1:T(1,128)S(1)}, s32[64,2048]{1,0:T(8,128)S(1)}, bf16[2048,1024]{1,0:T(8,128)(2,1)}, ...), branch_computations={%region_4.5_spmd, %region_5.8_spmd} | conditional | flops 2194280448 | bytes 75121424 | solution.py:97
  160.5 0.1 broadcast_compare_fusion
  160.7 6.6 %copy.64 = bf16[2048,1024]{0,1:T(8,128)(2,1)} copy(bf16[2048,1024]{1,0:T(8,128)(2,1)} %get-tuple-element.70) | data formatting | bytes 8388608 | tf_op jit(solution)/shard_map
  167.2 2.5 fusion.36
  169.8 7.8 %select_reduce_fusion = (f32[4,64,8]{2,1,0:T(8,128)S(1)}, f32[4,64,8,2048]{3,2,1,0:T(8,128)}) fusion(pred[64,2048]{1,0:T(8,128)(4,1)S(1)} %broadcast_compare_fusion, bf16[2048,4,128,1]{0,2,3,1:T(8,128)(2,1)S(1)} %bitcast.69, bf16[64,4,8,128]{3,2,1,0:T(8,128)(2,1)S(1)} %get-tuple-element.71), kind=kOutput, calls=%fused_computation.2 | convolution fusion | flops 1086322688 | bytes 19537920 | tf_op jit(solution)/shard_map/cond/branch_1_fun/rgjd,ngd->grjn/dot_general | solution.py:56
  177.6 0.1 copy.66
  177.7 8.3 %fusion.1 = f32[4,64,8]{2,1,0:T(8,128)S(1)} fusion(f32[4,64,8,2048]{3,2,1,0:T(8,128)} %get-tuple-element.80, f32[4,64,8]{2,1,0:T(8,128)S(1)} %max.2, pred[64,2048]{1,0:T(8,128)(4,1)S(1)} %broadcast_compare_fusion), kind=kLoop, calls=%fused_computation.4 | loop fusion | flops 16775168 | bytes 16924672 | tf_op jit(solution)/shard_map/cond/branch_1_fun/reduce_sum | solution.py:63
  186.0 0.1 copy.67
  186.1 9.3 %fusion.5 = f32[4,64,8,128]{3,2,1,0:T(8,128)} fusion(bf16[2048,4,128,1]{0,2,3,1:T(8,128)(2,1)S(1)} %bitcast.76, f32[4,64,8,2048]{3,2,1,0:T(8,128)} %get-tuple-element.80, f32[4,64,8]{2,1,0:T(8,128)S(1)} %max.2, pred[64,2048]{1,0:T(8,128)(4,1)S(1)} %broadcast_compare_fusion, f32[4,64,8,128]{3,2,1,0:T(8,128)} %get-tuple-element.32, ...), kind=kOutput, calls=%fused_computation.7 | convolution fusion | flops 1091043328 | bytes 21118976 | tf_op jit(solution)/shard_map/cond/branch_1_fun/grjn,ngd->grjd/dot_general | solution.py:64
  195.4 1.6 divide_bitcast_fusion
  197.0 0.1 copy.68
  197.1 0.2 reshape.140
  197.4 0.1 fusion.28
  197.5 3.4 %collective-permute-start = (bf16[1,64,4096]{2,1,0:T(8,128)(2,1)S(1)}, bf16[1,64,4096]{2,1,0:T(8,128)(2,1)S(1)}, u32[]{:S(2)}, u32[]{:S(2)}) collective-permute-start(bf16[1,64,4096]{2,1,0:T(8,128)(2,1)S(1)} %fusion.28), channel_id=1, source_target_pairs={{480,0},{0,32},{32,64},{64,96},{96,128},{128,160},{160,192},{192,2... | collective-permute-start | bytes 1572872 | tf_op jit(solution)/shard_map/ppermute | solution.py:15
  200.8 0.1 copy.62
  200.9 0.7 convert_element_type.67
  201.7 51.6 %collective-permute-done = bf16[1,64,4096]{2,1,0:T(8,128)(2,1)S(1)} collective-permute-done((bf16[1,64,4096]{2,1,0:T(8,128)(2,1)S(1)}, bf16[1,64,4096]{2,1,0:T(8,128)(2,1)S(1)}, u32[]{:S(2)}, u32[]{:S(2)}) %collective-permute-start) | collective-permute-done | bytes 524320 | tf_op jit(solution)/shard_map/ppermute | solution.py:15
  253.3 0.8 copy.108
  (23 shorter events, 0.2 us)
Async XLA Ops:
  7.2 5.7 %copy-start = (bf16[1,64,4096]{2,1,0:T(8,128)(2,1)S(1)}, bf16[1,64,4096]{2,1,0:T(8,128)(2,1)}, u32[]{:S(2)}) copy-start(bf16[1,64,4096]{2,1,0:T(8,128)(2,1)} %param.9) | copy-start | bytes 1572868
  7.2 5.4 %copy-start.3 = (bf16[1,4096]{1,0:T(2,128)(2,1)S(1)}, bf16[1,4096]{1,0:T(2,128)(2,1)}, u32[]{:S(2)}) copy-start(bf16[1,4096]{1,0:T(2,128)(2,1)} %param.10) | copy-start | bytes 24580
  7.2 5.5 %copy-start.4 = (s32[1,8]{1,0:T(1,128)S(1)}, s32[1,8]{1,0:T(1,128)}, u32[]{:S(2)}) copy-start(s32[1,8]{1,0:T(1,128)} %param.15) | copy-start | bytes 100
  7.2 76.3 %all-gather.3.cloned.1.call-start = ((), (), s32[]{:S(2)}) async-start(), calls=%async_computation | async-start | bytes 6488064 | tf_op jit(solution)/shard_map/all_gather | solution.py:79
  9.7 150.7 %all-gather.5.cloned.1.call-start = ((), (), s32[]{:S(2)}) async-start(), calls=%async_computation.1 | async-start | bytes 4325376 | tf_op jit(solution)/shard_map/all_gather | solution.py:94
  90.1 3.7 %copy-start.2 = (bf16[1,64,4096]{2,1,0:T(8,128)(2,1)S(1)}, bf16[1,64,4096]{2,1,0:T(8,128)(2,1)}, u32[]{:S(2)}) copy-start(bf16[1,64,4096]{2,1,0:T(8,128)(2,1)} %param.11) | copy-start | bytes 1572868
  195.4 2.0 copy-start.1
  197.5 55.8 %collective-permute-start = (bf16[1,64,4096]{2,1,0:T(8,128)(2,1)S(1)}, bf16[1,64,4096]{2,1,0:T(8,128)(2,1)S(1)}, u32[]{:S(2)}, u32[]{:S(2)}) collective-permute-start(bf16[1,64,4096]{2,1,0:T(8,128)(2,1)S(1)} %fusion.28), channel_id=1, source_target_pairs={{480,0},{0,32},{32,64},{64,96},{96,128},{128,160},{160,192},{192,2... | collective-permute-start | bytes 1572872 | tf_op jit(solution)/shard_map/ppermute | solution.py:15
Sparse Core Ops, SparseCore 0:
  10.7 72.7 all-gather.2
  93.9 66.5 all-gather.4
where the time goes:
time: 262 us; the launch traced here: 261 us
  waiting for transfers between devices  178 us (68%)
  matrix products  24.9 us (10%)
  local copies, waits for them, and re-layouts  21.7 us (8%)
  other arithmetic  18 us (7%)
  between operations  14.3 us (5%)
  starting transfers between devices  3.46 us (1%)
    all_gather x1, waiting for transfers between devices, local(): lax.all_gather(packed, 'zero', axis=0, tiled=True)  68.7 us
    all_gather x1, waiting for transfers between devices, local(): portion = lax.all_gather(kv_new, 'zero', axis=0, tiled=True)  58.1 us
    ppermute x1, waiting for transfers between devices, passed_along(): return lax.ppermute(block, axis, route)  51.6 us
    dot_general x2, matrix products, absorb(): jnp.einsum('grjn,ngd->grjd', weights.astype(jnp.bfloat16), value_grid, pr...  12.7 us
    dot_general x2, matrix products, absorb(): jnp.einsum('rgjd,ngd->grjn', query_grid, key_grid, preferred_element_type...  8.59 us
    reduce_sum x1, other arithmetic, absorb(): new_sum = run_sum * shrink + jnp.sum(weights, axis=-1)  8.27 us
    another operation x3, local copies, waits for them, and re-layouts  6.73 us
  transfers between devices with their start and end apart: 3, of which 3 were waited for; matrix products, arithmetic and copies ran while one was open for 5% of the time, Pallas kernels for 0%

commit v1 on v0

--- a/solution.py
+++ b/solution.py
@@ -76,9 +76,16 @@
     packed = jnp.concatenate(
         [panel_blocks[0].reshape(weight_rows, block_size), cache_local], axis=0
     )
-    gathered = lax.all_gather(packed, "zero", axis=0, tiled=True).reshape(
-        zero_size, packed.shape[0], block_size
+    press_sums_all = lambda u_in: jnp.concatenate(
+        lax.all_to_all(
+            jnp.stack([u_in for _ in range(lax.axis_size("zero"))]),
+            "zero",
+            split_axis=0,
+            concat_axis=0,
+        ),
+        axis=0,
     )
+    gathered = press_sums_all(packed).reshape(zero_size, packed.shape[0], block_size)
     all_blocks = gathered[:, :weight_rows].reshape(zero_size * local_slots, block_size, block_size)
     cache_portion = gathered[:, weight_rows:].reshape(
         zero_size * cached_kv.shape[1], cached_kv.shape[2]

time: 262 us -> 340 us (1.30)
  waiting for transfers between devices: 178 us -> 246 us
  starting transfers between devices: 3.46 us -> 12.8 us
    all_to_all x0 -> x1, waiting for transfers between devices: none -> 135 us  [local(): lax.all_to_all(jnp.stack([u_in for _ in range(lax.axis_size('zero'))]), '...]
    all_gather x1 -> x0, waiting for transfers between devices: 68.7 us -> none  [local(): lax.all_gather(packed, 'zero', axis=0, tiled=True)]
    all_to_all x0 -> x1, starting transfers between devices: none -> 9.33 us  [local(): lax.all_to_all(jnp.stack([u_in for _ in range(lax.axis_size('zero'))]), '...]
    another operation x3 -> x4, local copies, waits for them, and re-layouts: 6.73 us -> 10.8 us
  transfers between devices with their start and end apart: 3 -> 3, of which waited for: 3 -> 3; matrix products, arithmetic and copies ran while one was open for 5% -> 4% of each run, Pallas kernels for 0% -> 0%
where the time goes in v1:
time: 340 us; the launch traced here: 339 us
  waiting for transfers between devices  246 us (72%)
  matrix products  24.9 us (7%)
  local copies, waits for them, and re-layouts  24.4 us (7%)
  other arithmetic  16.3 us (5%)
  between operations  14.3 us (4%)
  starting transfers between devices  12.8 us (4%)
    all_to_all x1, waiting for transfers between devices, local(): lax.all_to_all(jnp.stack([u_in for _ in range(lax.axis_size('zero'))]), '...  135 us
    all_gather x1, waiting for transfers between devices, local(): portion = lax.all_gather(kv_new, 'zero', axis=0, tiled=True)  59.8 us
    ppermute x1, waiting for transfers between devices, passed_along(): return lax.ppermute(block, axis, route)  51.6 us
    dot_general x2, matrix products, absorb(): jnp.einsum('grjn,ngd->grjd', weights.astype(jnp.bfloat16), value_grid, pr...  12.7 us
    all_to_all x1, starting transfers between devices, local(): lax.all_to_all(jnp.stack([u_in for _ in range(lax.axis_size('zero'))]), '...  9.33 us
    dot_general x2, matrix products, absorb(): jnp.einsum('rgjd,ngd->grjn', query_grid, key_grid, preferred_element_type...  8.58 us
    reduce_sum x1, other arithmetic, absorb(): new_sum = run_sum * shrink + jnp.sum(weights, axis=-1)  8.27 us
  transfers between devices with their start and end apart: 3, of which 3 were waited for; matrix products, arithmetic and copies ran while one was open for 4% of the time, Pallas kernels for 0%

profile of v1, /device:TPU:96, one launch (start us, length us, event | category | flops | bytes accessed | tf_op | source)
XLA Modules:
  0.0 339.1 jit_solution(9160665678906860108)
XLA Ops:
  7.2 0.8 reshape_squeeze.15
  7.9 0.9 pad_maximum_fusion
  8.9 4.1 %stack.2 = bf16[32,768,128]{2,1,0:T(8,128)(2,1)} broadcast(bf16[768,128]{1,0:T(8,128)(2,1)S(1)} %pad_maximum_fusion), dimensions={1,2} | broadcast | bytes 6488064 | tf_op jit(solution)/shard_map/stack | solution.py:81
  13.0 9.3 %all-to-all-start = ((bf16[32,768,128]{2,1,0:T(8,128)(2,1)}), bf16[32,768,128]{2,1,0:T(8,128)(2,1)}, u32[]{:S(2)}, u32[]{:S(2)}) async-start(bf16[32,768,128]{2,1,0:T(8,128)(2,1)} %stack.2), calls=%async_computation | async-start | bytes 12582912 | tf_op jit(solution)/shard_map/all_to_all | solution.py:80
  22.3 0.0 all-gather.2.cloned.1.call-start
  22.4 0.1 reshape_squeeze.18
  22.4 0.1 reshape_squeeze.17
  22.5 0.1 convert_bitcast_fusion
  22.6 0.2 copy.84
  22.8 0.1 fusion.33
  22.9 0.1 reshape.141
  23.0 0.2 fusion.27
  23.2 0.7 fusion.30
  23.9 1.1 gather_fusion
  25.0 134.9 %all-to-all-done = bf16[32,768,128]{2,1,0:T(8,128)(2,1)} async-done(((bf16[32,768,128]{2,1,0:T(8,128)(2,1)}), bf16[32,768,128]{2,1,0:T(8,128)(2,1)}, u32[]{:S(2)}, u32[]{:S(2)}) %all-to-all-start) | async-done | bytes 6291488 | tf_op jit(solution)/shard_map/all_to_all | solution.py:80
  160.0 2.8 slice.29
  162.8 3.7 %broadcast_multiply_fusion = f32[160,128,64]{1,2,0:T(8,128)} fusion(f32[160]{0:T(256)S(1)} %reshape.141, bf16[160,128,128]{2,1,0:T(8,128)(2,1)S(1)} %bitcast.67, bf16[160,64,128]{2,1,0:T(8,128)(2,1)S(1)} %gather_fusion, pred[160]{0:T(512)(128)(4,1)S(1)} %compare_and_fusion), kind=kOutput, calls=%fused_computation.24 | convolution fusion | flops 338165760 | bytes 13108000 | tf_op jit(solution)/shard_map/rsk,skn->rsn/dot_general | solution.py:94
  166.5 3.0 reduce_sum.38
  169.5 0.7 copy_bitcast_fusion
  170.2 0.1 copy.83
  170.3 1.3 slice.26
  171.6 0.5 reshape.133
  172.1 0.1 fusion.37
  172.2 0.2 copy.54
  172.4 0.8 bitcast_reduce_fusion
  173.2 1.1 fusion.13
  174.3 0.1 copy.57
  174.4 1.0 copy.58
  175.4 3.4 %fusion.23 = f32[4,64,8,128]{3,2,1,0:T(8,128)} fusion(bf16[512,4,128,1]{0,2,3,1:T(8,128)(2,1)} %bitcast.75, bf16[4,64,8,512]{3,1,2,0:T(8,128)(2,1)S(1)} %get-tuple-element.81, f32[4,64,8]{2,1,0:T(8,128)S(1)} %copy.57), kind=kOutput, calls=%fused_computation.31 | convolution fusion | flops 268697600 | bytes 3678208 | tf_op jit(solution)/shard_map/grjn,ngd->grjd/dot_general | solution.py:64
  178.8 59.8 %all-gather.2.cloned.1.call-done = bf16[2048,1024]{1,0:T(8,128)(2,1)} async-done(((bf16[64,1024]{1,0:T(8,128)(2,1)}), bf16[2048,1024]{1,0:T(8,128)(2,1)}) %all-gather.2.cloned.1.call-update) | async-done | bytes 4194320 | tf_op jit(solution)/shard_map/all_gather | solution.py:101
  238.7 34.9 %conditional.1 = (f32[4,64,8]{2,1,0:T(8,128)S(1)}, f32[4,64,8,128]{3,2,1,0:T(8,128)}) conditional(s32[]{:T(128)} %convert_element_type.57, (f32[4,64,8]{1,2,0:T(8,128)S(1)}, f32[4,64,8,128]{3,2,1,0:T(8,128)}) %tuple.15, (s32[]{:T(128)}, s32[64,1]{0,1:T(1,128)S(1)}, s32[64,2048]{1,0:T(8,128)S(1)}, bf16[2048,1024]{1,0:T(8,128)(2,1)}, ...), branch_computations={%region_4.5_spmd, %region_5.8_spmd} | conditional | flops 2194280448 | bytes 75121424 | solution.py:104
  238.7 0.1 broadcast_compare_fusion
  238.9 6.6 %copy.64 = bf16[2048,1024]{0,1:T(8,128)(2,1)} copy(bf16[2048,1024]{1,0:T(8,128)(2,1)} %get-tuple-element.70) | data formatting | bytes 8388608 | tf_op jit(solution)/shard_map
  245.4 2.5 fusion.36
  248.0 7.8 %select_reduce_fusion = (f32[4,64,8]{2,1,0:T(8,128)S(1)}, f32[4,64,8,2048]{3,2,1,0:T(8,128)}) fusion(pred[64,2048]{1,0:T(8,128)(4,1)S(1)} %broadcast_compare_fusion, bf16[2048,4,128,1]{0,2,3,1:T(8,128)(2,1)S(1)} %bitcast.68, bf16[64,4,8,128]{3,2,1,0:T(8,128)(2,1)S(1)} %get-tuple-element.71), kind=kOutput, calls=%fused_computation.2 | convolution fusion | flops 1086322688 | bytes 19537920 | tf_op jit(solution)/shard_map/cond/branch_1_fun/rgjd,ngd->grjn/dot_general | solution.py:56
  255.8 0.1 copy.66
  255.9 8.3 %fusion.1 = f32[4,64,8]{2,1,0:T(8,128)S(1)} fusion(f32[4,64,8,2048]{3,2,1,0:T(8,128)} %get-tuple-element.80, f32[4,64,8]{2,1,0:T(8,128)S(1)} %max.2, pred[64,2048]{1,0:T(8,128)(4,1)S(1)} %broadcast_compare_fusion), kind=kLoop, calls=%fused_computation.4 | loop fusion | flops 16775168 | bytes 16924672 | tf_op jit(solution)/shard_map/cond/branch_1_fun/reduce_sum | solution.py:63
  264.2 0.1 copy.67
  264.3 9.3 %fusion.5 = f32[4,64,8,128]{3,2,1,0:T(8,128)} fusion(bf16[2048,4,128,1]{0,2,3,1:T(8,128)(2,1)S(1)} %bitcast.73, f32[4,64,8,2048]{3,2,1,0:T(8,128)} %get-tuple-element.80, f32[4,64,8]{2,1,0:T(8,128)S(1)} %max.2, pred[64,2048]{1,0:T(8,128)(4,1)S(1)} %broadcast_compare_fusion, f32[4,64,8,128]{3,2,1,0:T(8,128)} %get-tuple-element.32, ...), kind=kOutput, calls=%fused_computation.7 | convolution fusion | flops 1091043328 | bytes 21118976 | tf_op jit(solution)/shard_map/cond/branch_1_fun/grjn,ngd->grjd/dot_general | solution.py:64
  273.6 1.6 divide_bitcast_fusion
  275.2 0.1 copy.68
  275.3 0.2 reshape.138
  275.5 0.1 fusion.28
  275.6 3.4 collective-permute-start
  279.0 0.1 copy.62
  279.1 0.7 convert_element_type.67
  279.8 51.6 %collective-permute-done = bf16[1,64,4096]{2,1,0:T(8,128)(2,1)S(1)} collective-permute-done((bf16[1,64,4096]{2,1,0:T(8,128)(2,1)S(1)}, bf16[1,64,4096]{2,1,0:T(8,128)(2,1)S(1)}, u32[]{:S(2)}, u32[]{:S(2)}) %collective-permute-start) | collective-permute-done | bytes 524320 | tf_op jit(solution)/shard_map/ppermute | solution.py:15
  331.5 0.8 copy.108
  (25 shorter events, 0.2 us)
Async XLA Ops:
  12.9 9.4 %copy-start.3 = (s32[1,8,20]{2,1,0:T(8,128)S(1)}, s32[1,8,20]{2,1,0:T(8,128)}, u32[]{:S(2)}) copy-start(s32[1,8,20]{2,1,0:T(8,128)} %param.14) | copy-start | bytes 1924
  12.9 9.6 %copy-start = (bf16[1,64,4096]{2,1,0:T(8,128)(2,1)S(1)}, bf16[1,64,4096]{2,1,0:T(8,128)(2,1)}, u32[]{:S(2)}) copy-start(bf16[1,64,4096]{2,1,0:T(8,128)(2,1)} %param.9) | copy-start | bytes 1572868
  12.9 9.8 %copy-start.4 = (bf16[1,4096]{1,0:T(2,128)(2,1)S(1)}, bf16[1,4096]{1,0:T(2,128)(2,1)}, u32[]{:S(2)}) copy-start(bf16[1,4096]{1,0:T(2,128)(2,1)} %param.10) | copy-start | bytes 24580
  13.0 9.9 %copy-start.5 = (s32[1,8]{1,0:T(1,128)S(1)}, s32[1,8]{1,0:T(1,128)}, u32[]{:S(2)}) copy-start(s32[1,8]{1,0:T(1,128)} %param.15) | copy-start | bytes 100
  13.0 147.0 %all-to-all-start = ((bf16[32,768,128]{2,1,0:T(8,128)(2,1)}), bf16[32,768,128]{2,1,0:T(8,128)(2,1)}, u32[]{:S(2)}, u32[]{:S(2)}) async-start(bf16[32,768,128]{2,1,0:T(8,128)(2,1)} %stack.2), calls=%async_computation | async-start | bytes 12582912 | tf_op jit(solution)/shard_map/all_to_all | solution.py:80
  22.3 216.3 %all-gather.2.cloned.1.call-start = ((), (), s32[]{:S(2)}) async-start(), calls=%async_computation.1 | async-start | bytes 4325376 | tf_op jit(solution)/shard_map/all_gather | solution.py:101
  166.5 3.7 %copy-start.2 = (bf16[1,64,4096]{2,1,0:T(8,128)(2,1)S(1)}, bf16[1,64,4096]{2,1,0:T(8,128)(2,1)}, u32[]{:S(2)}) copy-start(bf16[1,64,4096]{2,1,0:T(8,128)(2,1)} %param.11) | copy-start | bytes 1572868
  273.6 2.0 copy-start.1
  275.6 55.8 %collective-permute-start = (bf16[1,64,4096]{2,1,0:T(8,128)(2,1)S(1)}, bf16[1,64,4096]{2,1,0:T(8,128)(2,1)S(1)}, u32[]{:S(2)}, u32[]{:S(2)}) collective-permute-start(bf16[1,64,4096]{2,1,0:T(8,128)(2,1)S(1)} %fusion.28), channel_id=1, source_target_pairs={{480,0},{0,32},{32,64},{64,96},{96,128},{128,160},{160,192},{192,2... | collective-permute-start | bytes 1572872 | tf_op jit(solution)/shard_map/ppermute | solution.py:15
Sparse Core Ops, SparseCore 0:
  170.3 68.2 all-gather.1
